TPU v7x, 256 devices: a whole 4x4x8 slice. The times are simulated.
256 devices in a mesh: blk: 32 (over x, y, z_hi), head: 8 (over z_lo, core).
Axes of the slice: x: 4, y: 4, z: 8 (z_hi: 2, z_lo: 4; z = z_hi * 4 + z_lo), core: 2. Of those that a mesh axis runs over, the one named last changes fastest.
Arguments:
- tokens: bfloat16 [16384, 1408], P('blk'), may hold values from -6 to 6
- group_segment: int32 [4096], P('blk'), may hold values from 0 to 15, never falling along the last dimension, each value on 1 to 512 neighbouring positions
- ln1_gain: float32 [1408], replicated, may hold values from 0.1 to 1.9
- ln1_bias: float32 [1408], replicated, may hold values from -3 to 3
- qkv_weight: bfloat16 [1408, 3, 1408], P(None, None, 'head'), may hold values from -1 to 1
- out_weight: bfloat16 [1408, 1408], P('head'), may hold values from -0.15625 to 0.15625
- ln2_gain: float32 [1408], replicated, may hold values from 0.1 to 1.9
- ln2_bias: float32 [1408], replicated, may hold values from -3 to 3
- fc1_weight: bfloat16 [1408, 6144], P(None, 'head'), may hold values from -0.15625 to 0.15625
- fc2_weight: bfloat16 [6144, 1408], P('head'), may hold values from -0.078125 to 0.078125
- proj_weight: bfloat16 [5632, 4096], P('blk', 'head'), may hold values from -0.078125 to 0.078125
Outputs:
- merged_out: bfloat16 [4096, 4096], P('blk', 'head')
- req_rms: float32 [16], replicated
- req_peak: float32 [16], replicated
Inputs may be any that keep to these rules, and one draw needn't show every extreme that they name: `group_segment`: ids never fall along the rows; every request holds 1 to 512 groups, and one holds exactly that many.
All inputs are finite; a program needn't handle non-finite values.
Results may differ from a plain program's by a relative error of at most 0.017.
Values may be sent and summed in bfloat16 or wider, within the bound.
No kernel may reach another device: no remote copies, remote signals or barrier semaphores. Data moves between devices by JAX's collectives and lax.ppermute only.
A program may use at most 64 MiB of HBM per device.

v0:
```python
import jax
import jax.numpy as jnp
from jax import lax
from jax.sharding import PartitionSpec as P

HD = 88
OUTW = 4096
REACH = 4


def passed_along(x, axis, by):
    size = lax.axis_size(axis)
    pairs = [(i, i + by) for i in range(size) if 0 <= i + by < size]
    return lax.ppermute(x, axis, pairs)


def layer_norm(x, gain, bias):
    mean = jnp.mean(x, axis=-1, keepdims=True)
    var = jnp.mean((x - mean) ** 2, axis=-1, keepdims=True)
    return (x - mean) * lax.rsqrt(var + 1e-06) * gain + bias


def per_device(
    tokens,
    group_segment,
    ln1_gain,
    ln1_bias,
    qkv_weight,
    out_weight,
    ln2_gain,
    ln2_bias,
    fc1_weight,
    fc2_weight,
    proj_weight,
):
    rows = tokens.shape[0]
    x_in = tokens.astype(jnp.float32)
    seg_ids = jnp.repeat(group_segment + 1, 4)
    own_low = jnp.min(seg_ids)
    own_high = jnp.max(seg_ids)
    normed = layer_norm(x_in, ln1_gain, ln1_bias).astype(jnp.bfloat16)
    qkv = jnp.einsum("rd,dck->crk", normed, qkv_weight, preferred_element_type=jnp.float32).astype(
        jnp.bfloat16
    )
    local_heads = qkv.shape[2] // HD
    query = qkv[0].reshape(rows, local_heads, HD)
    keys = qkv[1]
    values = qkv[2]
    scale = 1.0 / HD**0.5

    def update(carry, piece):
        top, total, acc = carry
        kpiece, vpiece, ipiece = piece
        count = kpiece.shape[0]
        scores = (
            jnp.einsum(
                "rhe,phe->hrp",
                query,
                kpiece.reshape(count, local_heads, HD),
                preferred_element_type=jnp.float32,
            )
            * scale
        )
        mask = (seg_ids[:, None] == ipiece[None, :])[None]
        new_top = jnp.maximum(top, jnp.max(jnp.where(mask, scores, -1e30), axis=-1))
        factor = jnp.exp(top - new_top)
        weights = jnp.where(mask, jnp.exp(scores - new_top[..., None]), 0.0)
        total = total * factor + jnp.sum(weights, axis=-1)
        acc = acc * factor[..., None] + jnp.einsum(
            "hrp,phe->hre",
            weights.astype(jnp.bfloat16),
            vpiece.reshape(count, local_heads, HD),
            preferred_element_type=jnp.float32,
        )
        return (new_top, total, acc)

    def fold_block(carry, piece):
        ipiece = piece[2]
        touches = (jnp.min(ipiece) <= own_high) & (jnp.max(ipiece) >= own_low)
        return lax.cond(touches, lambda c: update(c, piece), lambda c: c, carry)

    start_state = (
        jnp.full((local_heads, rows), -1e30, jnp.float32),
        jnp.zeros((local_heads, rows), jnp.float32),
        jnp.zeros((local_heads, rows, HD), jnp.float32),
    )
    state = fold_block(start_state, (keys, values, seg_ids))
    for distance in range(1, REACH + 1):
        for offset in (distance, -distance):
            piece = passed_along((keys, values, seg_ids), "blk", offset)
            state = fold_block(state, piece)
    top, total, acc = state
    attn = (acc / total[..., None]).astype(jnp.bfloat16)
    attn = jnp.transpose(attn, (1, 0, 2)).reshape(rows, local_heads * HD)
    attn_part = jnp.dot(attn, out_weight, preferred_element_type=jnp.float32)
    h_one = x_in + lax.psum(attn_part.astype(jnp.bfloat16), "head").astype(jnp.float32)
    n_two = layer_norm(h_one, ln2_gain, ln2_bias).astype(jnp.bfloat16)
    hidden = jax.nn.gelu(
        jnp.dot(n_two, fc1_weight, preferred_element_type=jnp.float32), approximate=False
    ).astype(jnp.bfloat16)
    mlp_part = jnp.dot(hidden, fc2_weight, preferred_element_type=jnp.float32)
    layer = (h_one + lax.psum(mlp_part.astype(jnp.bfloat16), "head").astype(jnp.float32)).astype(
        jnp.bfloat16
    )
    grouped = layer.reshape(rows // 4, 4 * layer.shape[1])
    proj = jnp.dot(
        grouped,
        lax.all_gather(proj_weight, "blk", axis=0, tiled=True),
        preferred_element_type=jnp.float32,
    )
    requests = lax.axis_size("blk") // 2
    onehot = (group_segment[:, None] == jnp.arange(requests, dtype=jnp.int32)[None, :]).astype(
        jnp.float32
    )
    row_sq = jnp.sum(proj * proj, axis=1)
    local_sq = jnp.dot(row_sq, onehot, precision=lax.Precision.HIGHEST)
    local_count = jnp.sum(onehot, axis=0)
    tot_sq, tot_count = lax.psum((local_sq, local_count), ("blk", "head"))
    counts = tot_count / lax.axis_size("head")
    req_rms = jnp.sqrt(tot_sq / (counts * OUTW) + 1e-06)
    row_top = jnp.max(jnp.abs(proj), axis=1)
    local_peak = jnp.max(jnp.where(onehot > 0.0, row_top[:, None], 0.0), axis=0)
    req_peak = lax.pmax(local_peak, ("blk", "head"))
    row_rms = jnp.dot(onehot, req_rms, precision=lax.Precision.HIGHEST)
    merged_out = (proj / row_rms[:, None]).astype(jnp.bfloat16)
    return (merged_out, req_rms, req_peak)


def solution(mesh):
    placed = (
        P("blk", None),
        P("blk"),
        P(),
        P(),
        P(None, None, "head"),
        P("head", None),
        P(),
        P(),
        P(None, "head"),
        P("head", None),
        P("blk", "head"),
    )
    return jax.shard_map(
        per_device,
        mesh=mesh,
        in_specs=placed,
        out_specs=(P("blk", "head"), P(), P()),
        check_vma=False,
    )
```

profile of v0, /device:TPU:2, one launch (start us, length us, event | category | flops | bytes accessed | tf_op | source)
XLA Modules:
  0.0 587.5 jit_solution(7077625534504535688)
XLA Ops:
  9.1 9.2 %collective-permute-start.7 = (s32[512]{0:T(512)S(1)}, s32[512]{0:T(512)S(1)}, u32[]{:S(2)}, u32[]{:S(2)}) collective-permute-start(s32[512]{0:T(512)S(1)} %reshape.391), channel_id=1, source_target_pairs={{0,8},{8,16},{16,24},{24,32},{32,40},{40,48},{48,56},{56,64},{64,7... | collective-permute-start | bytes 6152 | tf_op jit(solution)/shard_map/ppermute | solution.py:14
  18.3 4.3 collective-permute-start.6
  24.6 6.0 %collective-permute-start.4 = (s32[512]{0:T(512)S(1)}, s32[512]{0:T(512)S(1)}, u32[]{:S(2)}, u32[]{:S(2)}) collective-permute-start(s32[512]{0:T(512)S(1)} %reshape.391), channel_id=1, source_target_pairs={{16,0},{24,8},{32,16},{40,24},{48,32},{56,40},{64,48},{72,56},{80,... | collective-permute-start | bytes 6152 | tf_op jit(solution)/shard_map/ppermute | solution.py:14
  30.6 4.3 collective-permute-start.3
  44.0 4.8 conditional.9
  48.9 3.5 collective-permute-start.8
  53.1 11.2 %collective-permute-start.2 = (s32[512]{0:T(512)S(1)}, s32[512]{0:T(512)S(1)}, u32[]{:S(2)}, u32[]{:S(2)}) collective-permute-start(s32[512]{0:T(512)S(1)} %reshape.391), channel_id=1, source_target_pairs={{24,0},{32,8},{40,16},{48,24},{56,32},{64,40},{72,48},{80,56},{88,... | collective-permute-start | bytes 6152 | tf_op jit(solution)/shard_map/ppermute | solution.py:14
  66.3 6.3 %collective-permute-start = (s32[512]{0:T(512)S(1)}, s32[512]{0:T(512)S(1)}, u32[]{:S(2)}, u32[]{:S(2)}) collective-permute-start(s32[512]{0:T(512)S(1)} %reshape.391), channel_id=1, source_target_pairs={{32,0},{40,8},{48,16},{56,24},{64,32},{72,40},{80,48},{88,56},{96,... | collective-permute-start | bytes 6152 | tf_op jit(solution)/shard_map/ppermute | solution.py:14
  78.5 2.8 collective-permute-start.10
  81.3 6.9 %collective-permute-start.9 = (bf16[512,176]{0,1:T(8,128)(2,1)S(1)}, bf16[512,176]{0,1:T(8,128)(2,1)}, u32[]{:S(2)}, u32[]{:S(2)}) collective-permute-start(bf16[512,176]{0,1:T(8,128)(2,1)S(1)} %get-tuple-element.365), channel_id=1, source_target_pairs={{0,8},{8,16},{16,24},{24,32},{32,40},{40,48},{48,56},{56,64},{64,7... | collective-permute-start | bytes 540680 | tf_op jit(solution)/shard_map/ppermute | solution.py:14
  88.3 5.8 collective-permute-start.11
  104.5 6.0 %collective-permute-start.14 = (bf16[512,176]{0,1:T(8,128)(2,1)S(1)}, bf16[512,176]{0,1:T(8,128)(2,1)}, u32[]{:S(2)}, u32[]{:S(2)}) collective-permute-start(bf16[512,176]{0,1:T(8,128)(2,1)S(1)} %get-tuple-element.366), channel_id=1, source_target_pairs={{16,0},{24,8},{32,16},{40,24},{48,32},{56,40},{64,48},{72,56},{80,... | collective-permute-start | bytes 540680 | tf_op jit(solution)/shard_map/ppermute | solution.py:14
  110.6 3.9 collective-permute-start.15
  114.5 3.4 collective-permute-start.16
  117.9 6.2 %collective-permute-start.17 = (bf16[512,176]{0,1:T(8,128)(2,1)S(1)}, bf16[512,176]{0,1:T(8,128)(2,1)}, u32[]{:S(2)}, u32[]{:S(2)}) collective-permute-start(bf16[512,176]{0,1:T(8,128)(2,1)S(1)} %get-tuple-element.365), channel_id=1, source_target_pairs={{0,24},{8,32},{16,40},{24,48},{32,56},{40,64},{48,72},{56,80},{64,... | collective-permute-start | bytes 540680 | tf_op jit(solution)/shard_map/ppermute | solution.py:14
  124.1 6.9 %collective-permute-start.18 = (bf16[512,176]{0,1:T(8,128)(2,1)S(1)}, bf16[512,176]{0,1:T(8,128)(2,1)}, u32[]{:S(2)}, u32[]{:S(2)}) collective-permute-start(bf16[512,176]{0,1:T(8,128)(2,1)S(1)} %get-tuple-element.366), channel_id=1, source_target_pairs={{24,0},{32,8},{40,16},{48,24},{56,32},{64,40},{72,48},{80,56},{88,... | collective-permute-start | bytes 540680 | tf_op jit(solution)/shard_map/ppermute | solution.py:14
  137.5 7.9 %collective-permute-start.19 = (bf16[512,176]{0,1:T(8,128)(2,1)S(1)}, bf16[512,176]{0,1:T(8,128)(2,1)}, u32[]{:S(2)}, u32[]{:S(2)}) collective-permute-start(bf16[512,176]{0,1:T(8,128)(2,1)S(1)} %get-tuple-element.365), channel_id=1, source_target_pairs={{24,0},{32,8},{40,16},{48,24},{56,32},{64,40},{72,48},{80,56},{88,... | collective-permute-start | bytes 540680 | tf_op jit(solution)/shard_map/ppermute | solution.py:14
  147.5 5.7 collective-permute-start.21
  155.8 6.0 %collective-permute-start.23 = (bf16[512,176]{0,1:T(8,128)(2,1)S(1)}, bf16[512,176]{0,1:T(8,128)(2,1)}, u32[]{:S(2)}, u32[]{:S(2)}) collective-permute-start(bf16[512,176]{0,1:T(8,128)(2,1)S(1)} %get-tuple-element.365), channel_id=1, source_target_pairs={{32,0},{40,8},{48,16},{56,24},{64,32},{72,40},{80,48},{88,56},{96,... | collective-permute-start | bytes 540680 | tf_op jit(solution)/shard_map/ppermute | solution.py:14
  168.3 6.0 %conditional.10 = ((f32[2,512]{1,0:T(2,128)}, f32[2,512]{1,0:T(2,128)S(1)}, f32[2,512,88]{1,2,0:T(8,128)S(1)})) conditional(s32[]{:T(128)} %convert_element_type.104, (f32[2,512]{1,0:T(2,128)}, f32[2,512]{1,0:T(2,128)S(1)}, f32[2,512,88]{1,2,0:T(8,128)S(1)}) %conditional.9, (s32[128,4]{1,0:T(8,128)S(1)}, s32[512]{0:T(512)S(1)}, ...), branch_computations={%region_24.25_spmd, %region_25.28_spmd} | conditional | flops 190760960 | bytes 8675360 | solution.py:80
  174.4 6.0 %conditional.11 = ((f32[2,512]{1,0:T(2,128)}, f32[2,512]{1,0:T(2,128)S(1)}, f32[2,512,88]{1,2,0:T(8,128)S(1)})) conditional(s32[]{:T(128)} %convert_element_type.103, (f32[2,512]{1,0:T(2,128)}, f32[2,512]{1,0:T(2,128)S(1)}, f32[2,512,88]{1,2,0:T(8,128)S(1)}) %get-tuple-element.423, (s32[128,4]{1,0:T(8,128)S(1)}, s32[512]{0:T(512)S(1)}, ...), branch_computations={%region_28.29_spmd, %region_29.32_spmd} | conditional | flops 190760960 | bytes 8675360 | solution.py:80
  180.4 6.0 %conditional.13 = ((f32[2,512]{1,0:T(2,128)}, f32[2,512]{1,0:T(2,128)S(1)}, f32[2,512,88]{1,2,0:T(8,128)S(1)})) conditional(s32[]{:T(128)} %convert_element_type.101, (f32[2,512]{1,0:T(2,128)}, f32[2,512]{1,0:T(2,128)S(1)}, f32[2,512,88]{1,2,0:T(8,128)S(1)}) %get-tuple-element.425, (s32[128,4]{1,0:T(8,128)S(1)}, s32[512]{0:T(512)S(1)}, ...), branch_computations={%region_36.37_spmd, %region_37.40_spmd} | conditional | flops 190760960 | bytes 8675360 | solution.py:80
  186.4 6.0 %conditional.15 = ((f32[2,512]{1,0:T(2,128)}, f32[2,512]{1,0:T(2,128)S(1)}, f32[2,512,88]{1,2,0:T(8,128)S(1)})) conditional(s32[]{:T(128)} %convert_element_type.99, (f32[2,512]{1,0:T(2,128)}, f32[2,512]{1,0:T(2,128)S(1)}, f32[2,512,88]{1,2,0:T(8,128)S(1)}) %get-tuple-element.427, (s32[128,4]{1,0:T(8,128)S(1)}, s32[512]{0:T(512)S(1)}, ...), branch_computations={%region_44.0_spmd, %region_45.48_spmd} | conditional | flops 190760960 | bytes 8675360 | solution.py:80
  193.1 5.6 conditional.17
  200.6 84.3 %all-reduce.4.cloned.1.call-done = bf16[512,1408]{1,0:T(8,128)(2,1)} async-done(((bf16[512,1408]{1,0:T(8,128)(2,1)}), bf16[512,1408]{1,0:T(8,128)(2,1)}) %all-reduce.4.cloned.1.call-update) | async-done | bytes 1441808 | tf_op jit(solution)/shard_map/psum | solution.py:96
  288.3 9.7 %convolution_convert_fusion = bf16[512,1408]{1,0:T(8,128)(2,1)} fusion(bf16[768,1408]{1,0:T(8,128)(2,1)S(1)} %copy-done, bf16[1408,768]{1,0:T(8,128)(2,1)} %param.37, bf16[512,1408]{1,0:T(8,128)(2,1)} %all-reduce.4.cloned.1.call-done, bf16[512,1408]{1,0:T(8,128)(2,1)} %param.29, f32[1408]{0:T(1024)S(1)} %copy-done.12, f32[1408]{0:T(1024)S(1)} %copy-done.13, ...), kind=kOutput, calls=%fused_computation.123 | convolution fusion | flops 2246639616 | bytes 8666112 | tf_op jit(solution)/shard_map/dot_general | solution.py:101
  298.6 105.5 %all-reduce.6.cloned.1.call-done = bf16[512,1408]{1,0:T(8,128)(2,1)} async-done(((bf16[512,1408]{1,0:T(8,128)(2,1)}), bf16[512,1408]{1,0:T(8,128)(2,1)}) %all-reduce.6.cloned.1.call-update) | async-done | bytes 1441808 | tf_op jit(solution)/shard_map/psum | solution.py:102
  404.1 4.0 add_convert_fusion
  408.2 3.6 reshape.393
  412.8 4.1 abs_reduce_fusion
  417.1 88.7 %all-reduce = (f32[16]{0:T(128)S(1)}, f32[16]{0:T(128)S(1)}) all-reduce(f32[16]{0:T(128)S(1)} %convolution_bitcast_fusion.1, f32[16]{0:T(128)S(1)} %get-tuple-element.324), channel_id=1, replica_groups=mesh['blk'=32,'head'=8] {'blk','head'}, use_global_device_ids=true, to_apply=%region_61.62 | all-reduce | flops 32 | bytes 256 | tf_op jit(solution)/shard_map/psum | solution.py:118
  506.0 73.3 %pmax.7 = f32[16]{0:T(128)} all-reduce(f32[16]{0:T(128)S(1)} %get-tuple-element.323), channel_id=1, replica_groups=mesh['blk'=32,'head'=8] {'blk','head'}, use_global_device_ids=true, to_apply=%region_66.67 | all-reduce | flops 16 | bytes 128 | tf_op jit(solution)/shard_map/pmax | solution.py:123
  (146 shorter events, 67.6 us)
Async XLA Ops:
  8.0 280.3 %copy-start = (bf16[768,1408]{1,0:T(8,128)(2,1)S(1)}, bf16[768,1408]{1,0:T(8,128)(2,1)}, u32[]{:S(2)}) copy-start(bf16[768,1408]{1,0:T(8,128)(2,1)} %param.38) | copy-start | bytes 6488068
  8.0 29.1 %copy-start.11 = (f32[1408]{0:T(1024)S(1)}, f32[1408]{0:T(1024)}, u32[]{:S(2)}) copy-start(f32[1408]{0:T(1024)} %param.31) | copy-start | bytes 16900
  8.0 29.1 %copy-start.10 = (f32[1408]{0:T(1024)S(1)}, f32[1408]{0:T(1024)}, u32[]{:S(2)}) copy-start(f32[1408]{0:T(1024)} %param.32) | copy-start | bytes 16900
  8.0 276.9 %all-reduce.4.cloned.1.call-start = ((), (), s32[]{:S(2)}) async-start(), calls=%async_computation | async-start | bytes 2883584 | tf_op jit(solution)/shard_map/psum | solution.py:96
  9.1 27.5 %copy-start.1 = (bf16[512,1408]{1,0:T(8,128)(2,1)S(1)}, bf16[512,1408]{1,0:T(8,128)(2,1)}, u32[]{:S(2)}) copy-start(bf16[512,1408]{1,0:T(8,128)(2,1)} %param.29) | copy-start | bytes 4325380
  9.1 39.8 %collective-permute-start.7 = (s32[512]{0:T(512)S(1)}, s32[512]{0:T(512)S(1)}, u32[]{:S(2)}, u32[]{:S(2)}) collective-permute-start(s32[512]{0:T(512)S(1)} %reshape.391), channel_id=1, source_target_pairs={{0,8},{8,16},{16,24},{24,32},{32,40},{40,48},{48,56},{56,64},{64,7... | collective-permute-start | bytes 6152 | tf_op jit(solution)/shard_map/ppermute | solution.py:14
  18.3 34.8 %collective-permute-start.6 = (s32[512]{0:T(512)S(1)}, s32[512]{0:T(512)S(1)}, u32[]{:S(2)}, u32[]{:S(2)}) collective-permute-start(s32[512]{0:T(512)S(1)} %reshape.391), channel_id=1, source_target_pairs={{8,0},{16,8},{24,16},{32,24},{40,32},{48,40},{56,48},{64,56},{72,6... | collective-permute-start | bytes 6152 | tf_op jit(solution)/shard_map/ppermute | solution.py:14
  22.7 41.7 %collective-permute-start.5 = (s32[512]{0:T(512)S(1)}, s32[512]{0:T(512)S(1)}, u32[]{:S(2)}, u32[]{:S(2)}) collective-permute-start(s32[512]{0:T(512)S(1)} %reshape.391), channel_id=1, source_target_pairs={{0,16},{8,24},{16,32},{24,40},{32,48},{40,56},{48,64},{56,72},{64,... | collective-permute-start | bytes 6152 | tf_op jit(solution)/shard_map/ppermute | solution.py:14
  24.6 41.7 %collective-permute-start.4 = (s32[512]{0:T(512)S(1)}, s32[512]{0:T(512)S(1)}, u32[]{:S(2)}, u32[]{:S(2)}) collective-permute-start(s32[512]{0:T(512)S(1)} %reshape.391), channel_id=1, source_target_pairs={{16,0},{24,8},{32,16},{40,24},{48,32},{56,40},{64,48},{72,56},{80,... | collective-permute-start | bytes 6152 | tf_op jit(solution)/shard_map/ppermute | solution.py:14
  30.6 47.8 %collective-permute-start.3 = (s32[512]{0:T(512)S(1)}, s32[512]{0:T(512)S(1)}, u32[]{:S(2)}, u32[]{:S(2)}) collective-permute-start(s32[512]{0:T(512)S(1)} %reshape.391), channel_id=1, source_target_pairs={{0,24},{8,32},{16,40},{24,48},{32,56},{40,64},{48,72},{56,80},{64,... | collective-permute-start | bytes 6152 | tf_op jit(solution)/shard_map/ppermute | solution.py:14
  48.9 47.2 %collective-permute-start.8 = (bf16[512,176]{0,1:T(8,128)(2,1)S(1)}, bf16[512,176]{0,1:T(8,128)(2,1)S(1)}, u32[]{:S(2)}, u32[]{:S(2)}) collective-permute-start(bf16[512,176]{0,1:T(8,128)(2,1)S(1)} %get-tuple-element.366), channel_id=1, source_target_pairs={{0,8},{8,16},{16,24},{24,32},{32,40},{40,48},{48,56},{56,64},{64,7... | collective-permute-start | bytes 540680 | tf_op jit(solution)/shard_map/ppermute | solution.py:14
  53.1 28.2 %collective-permute-start.2 = (s32[512]{0:T(512)S(1)}, s32[512]{0:T(512)S(1)}, u32[]{:S(2)}, u32[]{:S(2)}) collective-permute-start(s32[512]{0:T(512)S(1)} %reshape.391), channel_id=1, source_target_pairs={{24,0},{32,8},{40,16},{48,24},{56,32},{64,40},{72,48},{80,56},{88,... | collective-permute-start | bytes 6152 | tf_op jit(solution)/shard_map/ppermute | solution.py:14
  64.4 23.9 %collective-permute-start.1 = (s32[512]{0:T(512)S(1)}, s32[512]{0:T(512)S(1)}, u32[]{:S(2)}, u32[]{:S(2)}) collective-permute-start(s32[512]{0:T(512)S(1)} %reshape.391), channel_id=1, source_target_pairs={{0,32},{8,40},{16,48},{24,56},{32,64},{40,72},{48,80},{56,88},{64,... | collective-permute-start | bytes 6152 | tf_op jit(solution)/shard_map/ppermute | solution.py:14
  66.3 27.8 %collective-permute-start = (s32[512]{0:T(512)S(1)}, s32[512]{0:T(512)S(1)}, u32[]{:S(2)}, u32[]{:S(2)}) collective-permute-start(s32[512]{0:T(512)S(1)} %reshape.391), channel_id=1, source_target_pairs={{32,0},{40,8},{48,16},{56,24},{64,32},{72,40},{80,48},{88,56},{96,... | collective-permute-start | bytes 6152 | tf_op jit(solution)/shard_map/ppermute | solution.py:14
  78.5 32.1 %collective-permute-start.10 = (bf16[512,176]{0,1:T(8,128)(2,1)S(1)}, bf16[512,176]{0,1:T(8,128)(2,1)}, u32[]{:S(2)}, u32[]{:S(2)}) collective-permute-start(bf16[512,176]{0,1:T(8,128)(2,1)S(1)} %get-tuple-element.366), channel_id=1, source_target_pairs={{8,0},{16,8},{24,16},{32,24},{40,32},{48,40},{56,48},{64,56},{72,6... | collective-permute-start | bytes 540680 | tf_op jit(solution)/shard_map/ppermute | solution.py:14
  81.3 23.2 %collective-permute-start.9 = (bf16[512,176]{0,1:T(8,128)(2,1)S(1)}, bf16[512,176]{0,1:T(8,128)(2,1)}, u32[]{:S(2)}, u32[]{:S(2)}) collective-permute-start(bf16[512,176]{0,1:T(8,128)(2,1)S(1)} %get-tuple-element.365), channel_id=1, source_target_pairs={{0,8},{8,16},{16,24},{24,32},{32,40},{40,48},{48,56},{56,64},{64,7... | collective-permute-start | bytes 540680 | tf_op jit(solution)/shard_map/ppermute | solution.py:14
  88.3 26.3 %collective-permute-start.11 = (bf16[512,176]{0,1:T(8,128)(2,1)S(1)}, bf16[512,176]{0,1:T(8,128)(2,1)}, u32[]{:S(2)}, u32[]{:S(2)}) collective-permute-start(bf16[512,176]{0,1:T(8,128)(2,1)S(1)} %get-tuple-element.365), channel_id=1, source_target_pairs={{8,0},{16,8},{24,16},{32,24},{40,32},{48,40},{56,48},{64,56},{72,6... | collective-permute-start | bytes 540680 | tf_op jit(solution)/shard_map/ppermute | solution.py:14
  94.1 23.8 %collective-permute-start.12 = (bf16[512,176]{0,1:T(8,128)(2,1)S(1)}, bf16[512,176]{0,1:T(8,128)(2,1)}, u32[]{:S(2)}, u32[]{:S(2)}) collective-permute-start(bf16[512,176]{0,1:T(8,128)(2,1)S(1)} %get-tuple-element.366), channel_id=1, source_target_pairs={{0,16},{8,24},{16,32},{24,40},{32,48},{40,56},{48,64},{56,72},{64,... | collective-permute-start | bytes 540680 | tf_op jit(solution)/shard_map/ppermute | solution.py:14
  96.1 28.0 %collective-permute-start.13 = (bf16[512,176]{0,1:T(8,128)(2,1)S(1)}, bf16[512,176]{0,1:T(8,128)(2,1)}, u32[]{:S(2)}, u32[]{:S(2)}) collective-permute-start(bf16[512,176]{0,1:T(8,128)(2,1)S(1)} %get-tuple-element.365), channel_id=1, source_target_pairs={{0,16},{8,24},{16,32},{24,40},{32,48},{40,56},{48,64},{56,72},{64,... | collective-permute-start | bytes 540680 | tf_op jit(solution)/shard_map/ppermute | solution.py:14
  104.5 33.0 %collective-permute-start.14 = (bf16[512,176]{0,1:T(8,128)(2,1)S(1)}, bf16[512,176]{0,1:T(8,128)(2,1)}, u32[]{:S(2)}, u32[]{:S(2)}) collective-permute-start(bf16[512,176]{0,1:T(8,128)(2,1)S(1)} %get-tuple-element.366), channel_id=1, source_target_pairs={{16,0},{24,8},{32,16},{40,24},{48,32},{56,40},{64,48},{72,56},{80,... | collective-permute-start | bytes 540680 | tf_op jit(solution)/shard_map/ppermute | solution.py:14
  110.6 34.9 %collective-permute-start.15 = (bf16[512,176]{0,1:T(8,128)(2,1)S(1)}, bf16[512,176]{0,1:T(8,128)(2,1)}, u32[]{:S(2)}, u32[]{:S(2)}) collective-permute-start(bf16[512,176]{0,1:T(8,128)(2,1)S(1)} %get-tuple-element.365), channel_id=1, source_target_pairs={{16,0},{24,8},{32,16},{40,24},{48,32},{56,40},{64,48},{72,56},{80,... | collective-permute-start | bytes 540680 | tf_op jit(solution)/shard_map/ppermute | solution.py:14
  114.5 32.9 %collective-permute-start.16 = (bf16[512,176]{0,1:T(8,128)(2,1)S(1)}, bf16[512,176]{0,1:T(8,128)(2,1)S(1)}, u32[]{:S(2)}, u32[]{:S(2)}) collective-permute-start(bf16[512,176]{0,1:T(8,128)(2,1)S(1)} %get-tuple-element.366), channel_id=1, source_target_pairs={{0,24},{8,32},{16,40},{24,48},{32,56},{40,64},{48,72},{56,80},{64,... | collective-permute-start | bytes 540680 | tf_op jit(solution)/shard_map/ppermute | solution.py:14
  117.9 35.3 %collective-permute-start.17 = (bf16[512,176]{0,1:T(8,128)(2,1)S(1)}, bf16[512,176]{0,1:T(8,128)(2,1)}, u32[]{:S(2)}, u32[]{:S(2)}) collective-permute-start(bf16[512,176]{0,1:T(8,128)(2,1)S(1)} %get-tuple-element.365), channel_id=1, source_target_pairs={{0,24},{8,32},{16,40},{24,48},{32,56},{40,64},{48,72},{56,80},{64,... | collective-permute-start | bytes 540680 | tf_op jit(solution)/shard_map/ppermute | solution.py:14
  124.1 31.7 %collective-permute-start.18 = (bf16[512,176]{0,1:T(8,128)(2,1)S(1)}, bf16[512,176]{0,1:T(8,128)(2,1)}, u32[]{:S(2)}, u32[]{:S(2)}) collective-permute-start(bf16[512,176]{0,1:T(8,128)(2,1)S(1)} %get-tuple-element.366), channel_id=1, source_target_pairs={{24,0},{32,8},{40,16},{48,24},{56,32},{64,40},{72,48},{80,56},{88,... | collective-permute-start | bytes 540680 | tf_op jit(solution)/shard_map/ppermute | solution.py:14
  137.5 48.9 %collective-permute-start.19 = (bf16[512,176]{0,1:T(8,128)(2,1)S(1)}, bf16[512,176]{0,1:T(8,128)(2,1)}, u32[]{:S(2)}, u32[]{:S(2)}) collective-permute-start(bf16[512,176]{0,1:T(8,128)(2,1)S(1)} %get-tuple-element.365), channel_id=1, source_target_pairs={{24,0},{32,8},{40,16},{48,24},{56,32},{64,40},{72,48},{80,56},{88,... | collective-permute-start | bytes 540680 | tf_op jit(solution)/shard_map/ppermute | solution.py:14
  145.5 47.0 %collective-permute-start.20 = (bf16[512,176]{0,1:T(8,128)(2,1)S(1)}, bf16[512,176]{0,1:T(8,128)(2,1)}, u32[]{:S(2)}, u32[]{:S(2)}) collective-permute-start(bf16[512,176]{0,1:T(8,128)(2,1)S(1)} %get-tuple-element.366), channel_id=1, source_target_pairs={{0,32},{8,40},{16,48},{24,56},{32,64},{40,72},{48,80},{56,88},{64,... | collective-permute-start | bytes 540680 | tf_op jit(solution)/shard_map/ppermute | solution.py:14
  147.5 45.0 %collective-permute-start.21 = (bf16[512,176]{0,1:T(8,128)(2,1)S(1)}, bf16[512,176]{0,1:T(8,128)(2,1)}, u32[]{:S(2)}, u32[]{:S(2)}) collective-permute-start(bf16[512,176]{0,1:T(8,128)(2,1)S(1)} %get-tuple-element.365), channel_id=1, source_target_pairs={{0,32},{8,40},{16,48},{24,56},{32,64},{40,72},{48,80},{56,88},{64,... | collective-permute-start | bytes 540680 | tf_op jit(solution)/shard_map/ppermute | solution.py:14
  153.2 39.3 %collective-permute-start.22 = (bf16[512,176]{0,1:T(8,128)(2,1)S(1)}, bf16[512,176]{0,1:T(8,128)(2,1)S(1)}, u32[]{:S(2)}, u32[]{:S(2)}) collective-permute-start(bf16[512,176]{0,1:T(8,128)(2,1)S(1)} %get-tuple-element.366), channel_id=1, source_target_pairs={{32,0},{40,8},{48,16},{56,24},{64,32},{72,40},{80,48},{88,56},{96,... | collective-permute-start | bytes 540680 | tf_op jit(solution)/shard_map/ppermute | solution.py:14
  155.8 36.7 %collective-permute-start.23 = (bf16[512,176]{0,1:T(8,128)(2,1)S(1)}, bf16[512,176]{0,1:T(8,128)(2,1)}, u32[]{:S(2)}, u32[]{:S(2)}) collective-permute-start(bf16[512,176]{0,1:T(8,128)(2,1)S(1)} %get-tuple-element.365), channel_id=1, source_target_pairs={{32,0},{40,8},{48,16},{56,24},{64,32},{72,40},{80,48},{88,56},{96,... | collective-permute-start | bytes 540680 | tf_op jit(solution)/shard_map/ppermute | solution.py:14
  200.6 203.5 %all-reduce.6.cloned.1.call-start = ((), (), s32[]{:S(2)}) async-start(), calls=%async_computation.1 | async-start | bytes 2883584 | tf_op jit(solution)/shard_map/psum | solution.py:102
  298.0 114.8 %all-gather.2.cloned.1.call-start = ((), (), s32[]{:S(2)}) async-start(), calls=%async_computation.2 | async-start | bytes 5947392 | tf_op jit(solution)/shard_map/all_gather | solution.py:108
  505.8 74.2 %copy-start.14 = (f32[16]{0:T(128)}, f32[16]{0:T(128)S(1)}, u32[]{:S(2)}) copy-start(f32[16]{0:T(128)S(1)} %add_sqrt_fusion) | copy-start | bytes 196
  (10 other events, 45.7 us)
Sparse Core Ops, SparseCore 0:
  200.7 84.1 all-reduce.3
  298.2 105.9 all-reduce.5
Sparse Core Ops, SparseCore 1:
  301.9 110.8 all-gather.1
where the time goes:
time: 591 us; the launch traced here: 587 us
  waiting for transfers between devices  191 us (32%)
  blocking collectives  162 us (27%)
  starting transfers between devices  119 us (20%)
  between operations  39.6 us (7%)
  matrix products  36.3 us (6%)
  other arithmetic  30.3 us (5%)
  local copies, waits for them, and re-layouts  8.47 us (1%)
    ppermute x24, starting transfers between devices, passed_along(): return lax.ppermute(x, axis, pairs)  119 us
    psum x1, waiting for transfers between devices, per_device(): lax.psum(mlp_part.astype(jnp.bfloat16), 'head').astype(jnp.float32)  106 us
    psum x1, blocking collectives, per_device(): tot_sq, tot_count = lax.psum((local_sq, local_count), ('blk', 'head'))  88.7 us
    psum x1, waiting for transfers between devices, per_device(): lax.psum(attn_part.astype(jnp.bfloat16), 'head').astype(jnp.float32)  84.3 us
    pmax x1, blocking collectives, per_device(): req_peak = lax.pmax(local_peak, ('blk', 'head'))  73.3 us
  transfers between devices with their start and end apart: 27, of which 3 were waited for; matrix products, arithmetic and copies ran while one was open for 8% of the time, Pallas kernels for 0%

commit v1 on v0

--- a/solution.py
+++ b/solution.py
@@ -12,6 +12,27 @@
     size = lax.axis_size(axis)
     pairs = [(i, i + by) for i in range(size) if 0 <= i + by < size]
     return lax.ppermute(x, axis, pairs)
+
+
+def butterfly(summed, peak):
+    split = summed.shape[0]
+    both = jnp.concatenate([summed, peak])
+    for axis in ("head", "blk"):
+        size = lax.axis_size(axis)
+        if size & (size - 1):
+            both = jnp.concatenate(
+                [lax.psum(both[:split], axis), lax.pmax(both[split:], axis)]
+            )
+            continue
+        step = 1
+        while step < size:
+            pairs = [(i, i ^ step) for i in range(size)]
+            other = lax.ppermute(both, axis, pairs)
+            both = jnp.concatenate(
+                [both[:split] + other[:split], jnp.maximum(both[split:], other[split:])]
+            )
+            step *= 2
+    return both[:split], both[split:]
 
 
 def layer_norm(x, gain, bias):
@@ -85,9 +106,19 @@
         jnp.zeros((local_heads, rows, HD), jnp.float32),
     )
     state = fold_block(start_state, (keys, values, seg_ids))
+    width = keys.shape[1]
+    packed = jnp.concatenate(
+        [keys, values, seg_ids.astype(jnp.bfloat16)[:, None]], axis=1
+    )
+    packed = jnp.pad(packed, ((0, 0), (0, (-packed.shape[1]) % 128)))
     for distance in range(1, REACH + 1):
         for offset in (distance, -distance):
-            piece = passed_along((keys, values, seg_ids), "blk", offset)
+            got = passed_along(packed, "blk", offset)
+            piece = (
+                got[:, :width],
+                got[:, width : 2 * width],
+                got[:, 2 * width].astype(jnp.int32),
+            )
             state = fold_block(state, piece)
     top, total, acc = state
     attn = (acc / total[..., None]).astype(jnp.bfloat16)
@@ -115,12 +146,12 @@
     row_sq = jnp.sum(proj * proj, axis=1)
     local_sq = jnp.dot(row_sq, onehot, precision=lax.Precision.HIGHEST)
     local_count = jnp.sum(onehot, axis=0)
-    tot_sq, tot_count = lax.psum((local_sq, local_count), ("blk", "head"))
+    row_top = jnp.max(jnp.abs(proj), axis=1)
+    local_peak = jnp.max(jnp.where(onehot > 0.0, row_top[:, None], 0.0), axis=0)
+    summed, req_peak = butterfly(jnp.concatenate([local_sq, local_count]), local_peak)
+    tot_sq, tot_count = summed[:requests], summed[requests:]
     counts = tot_count / lax.axis_size("head")
     req_rms = jnp.sqrt(tot_sq / (counts * OUTW) + 1e-06)
-    row_top = jnp.max(jnp.abs(proj), axis=1)
-    local_peak = jnp.max(jnp.where(onehot > 0.0, row_top[:, None], 0.0), axis=0)
-    req_peak = lax.pmax(local_peak, ("blk", "head"))
     row_rms = jnp.dot(onehot, req_rms, precision=lax.Precision.HIGHEST)
     merged_out = (proj / row_rms[:, None]).astype(jnp.bfloat16)
     return (merged_out, req_rms, req_peak)

time: 591 us -> 429 us (0.73)
  blocking collectives: 162 us -> 0 us
  waiting for transfers between devices: 191 us -> 244 us
  starting transfers between devices: 119 us -> 69.7 us
  matrix products: 36.3 us -> 24.4 us
  other arithmetic: 30.3 us -> 39.3 us
    psum x1 -> x0, blocking collectives: 88.7 us -> none  [per_device(): tot_sq, tot_count = lax.psum((local_sq, local_count), ('blk', 'head'))]
    ppermute x24 -> x8, starting transfers between devices: 119 us -> 42.7 us  [passed_along(): return lax.ppermute(x, axis, pairs)]
    pmax x1 -> x0, blocking collectives: 73.3 us -> none  [per_device(): req_peak = lax.pmax(local_peak, ('blk', 'head'))]
    ppermute x0 -> x8, starting transfers between devices: none -> 26.7 us  [butterfly(): other = lax.ppermute(both, axis, pairs)]
    ppermute x0 -> x8, waiting for transfers between devices: none -> 22.4 us  [butterfly(): other = lax.ppermute(both, axis, pairs)]
    psum x1, waiting for transfers between devices: 84.3 us -> 105 us  [per_device(): lax.psum(attn_part.astype(jnp.bfloat16), 'head').astype(jnp.float32)]
    ppermute x24 -> x8, waiting for transfers between devices: 0.06 us -> 9.12 us  [passed_along(): return lax.ppermute(x, axis, pairs)]
    slice x0 -> x7, local copies, waits for them, and re-layouts: none -> 6.27 us  [the longest x6 6.19 us: per_device(): got[:, width:2 * width]]
  transfers between devices with their start and end apart: 27 -> 19, of which waited for: 3 -> 12; matrix products, arithmetic and copies ran while one was open for 8% -> 5% of each run, Pallas kernels for 0% -> 0%
where the time goes in v1:
time: 429 us; the launch traced here: 428 us
  waiting for transfers between devices  244 us (57%)
  starting transfers between devices  69.7 us (16%)
  other arithmetic  39.3 us (9%)
  between operations  37.7 us (9%)
  matrix products  24.4 us (6%)
  local copies, waits for them, and re-layouts  13.6 us (3%)
    psum x1, waiting for transfers between devices, per_device(): lax.psum(mlp_part.astype(jnp.bfloat16), 'head').astype(jnp.float32)  106 us
    psum x1, waiting for transfers between devices, per_device(): lax.psum(attn_part.astype(jnp.bfloat16), 'head').astype(jnp.float32)  105 us
    ppermute x8, starting transfers between devices, passed_along(): return lax.ppermute(x, axis, pairs)  42.7 us
    ppermute x8, starting transfers between devices, butterfly(): other = lax.ppermute(both, axis, pairs)  26.7 us
    ppermute x8, waiting for transfers between devices, butterfly(): other = lax.ppermute(both, axis, pairs)  22.4 us
    reduce_max x8, other arithmetic, fold_block(): touches = (jnp.min(ipiece) <= own_high) & (jnp.max(ipiece) >= own_low)  10.2 us
    dot_general x1, matrix products, per_device(): mlp_part = jnp.dot(hidden, fc2_weight, preferred_element_type=jnp.float32)  9.72 us
    ppermute x8, waiting for transfers between devices, passed_along(): return lax.ppermute(x, axis, pairs)  9.12 us
  transfers between devices with their start and end apart: 19, of which 12 were waited for; matrix products, arithmetic and copies ran while one was open for 5% of the time, Pallas kernels for 0%

profile of v1, /device:TPU:2, one launch (start us, length us, event | category | flops | bytes accessed | tf_op | source)
XLA Modules:
  0.0 428.4 jit_solution(278302053135970011)
XLA Ops:
  11.2 2.6 fusion.91
  14.9 9.1 %collective-permute-start.7 = (bf16[512,384]{0,1:T(8,128)(2,1)}, bf16[512,384]{0,1:T(8,128)(2,1)}, u32[]{:S(2)}, u32[]{:S(2)}) collective-permute-start(bf16[512,384]{0,1:T(8,128)(2,1)} %fusion.135), channel_id=1, source_target_pairs={{0,8},{8,16},{16,24},{24,32},{32,40},{40,48},{48,56},{56,64},{64,7... | collective-permute-start | bytes 1179656 | tf_op jit(solution)/shard_map/ppermute | solution.py:14
  24.0 4.3 %collective-permute-start.6 = (bf16[512,384]{0,1:T(8,128)(2,1)}, bf16[512,384]{0,1:T(8,128)(2,1)}, u32[]{:S(2)}, u32[]{:S(2)}) collective-permute-start(bf16[512,384]{0,1:T(8,128)(2,1)} %fusion.135), channel_id=1, source_target_pairs={{8,0},{16,8},{24,16},{32,24},{40,32},{48,40},{56,48},{64,56},{72,6... | collective-permute-start | bytes 1179656 | tf_op jit(solution)/shard_map/ppermute | solution.py:14
  28.4 1.9 collective-permute-start.5
  30.3 6.0 %collective-permute-start.4 = (bf16[512,384]{0,1:T(8,128)(2,1)}, bf16[512,384]{0,1:T(8,128)(2,1)}, u32[]{:S(2)}, u32[]{:S(2)}) collective-permute-start(bf16[512,384]{0,1:T(8,128)(2,1)} %fusion.135), channel_id=1, source_target_pairs={{16,0},{24,8},{32,16},{40,24},{48,32},{56,40},{64,48},{72,56},{80,... | collective-permute-start | bytes 1179656 | tf_op jit(solution)/shard_map/ppermute | solution.py:14
  36.4 4.3 %collective-permute-start.3 = (bf16[512,384]{0,1:T(8,128)(2,1)}, bf16[512,384]{0,1:T(8,128)(2,1)}, u32[]{:S(2)}, u32[]{:S(2)}) collective-permute-start(bf16[512,384]{0,1:T(8,128)(2,1)} %fusion.135), channel_id=1, source_target_pairs={{0,24},{8,32},{16,40},{24,48},{32,56},{40,64},{48,72},{56,80},{64,... | collective-permute-start | bytes 1179656 | tf_op jit(solution)/shard_map/ppermute | solution.py:14
  43.8 4.8 %conditional.9 = (f32[2,512]{1,0:T(2,128)}, f32[2,512]{1,0:T(2,128)S(1)}, f32[2,512,88]{1,2,0:T(8,128)S(1)}) conditional(s32[]{:T(128)} %convert_element_type.182, () %tuple.65, (s32[128,4]{1,0:T(8,128)S(1)}, bf16[1,512,176]{1,2,0:T(8,128)(2,1)S(1)}, bf16[512,2,88]{0,2,1:T(8,128)(2,1)S(1)}, bf16[1,512,176]{1,2,0:T(8,128)(2,1)S(1)}) %tuple.161), branch_computations={%region_20.21_spmd, %region_21.24_spmd} | conditional | flops 190672896 | bytes 8292376 | solution.py:101
  48.7 8.7 %collective-permute-start.2 = (bf16[512,384]{0,1:T(8,128)(2,1)}, bf16[512,384]{0,1:T(8,128)(2,1)}, u32[]{:S(2)}, u32[]{:S(2)}) collective-permute-start(bf16[512,384]{0,1:T(8,128)(2,1)} %fusion.135), channel_id=1, source_target_pairs={{24,0},{32,8},{40,16},{48,24},{56,32},{64,40},{72,48},{80,56},{88,... | collective-permute-start | bytes 1179656 | tf_op jit(solution)/shard_map/ppermute | solution.py:14
  58.8 1.9 collective-permute-start.1
  62.1 6.3 %collective-permute-start = (bf16[512,384]{0,1:T(8,128)(2,1)}, bf16[512,384]{0,1:T(8,128)(2,1)S(1)}, u32[]{:S(2)}, u32[]{:S(2)}) collective-permute-start(bf16[512,384]{0,1:T(8,128)(2,1)} %fusion.135), channel_id=1, source_target_pairs={{32,0},{40,8},{48,16},{56,24},{64,32},{72,40},{80,48},{88,56},{96,... | collective-permute-start | bytes 1179656 | tf_op jit(solution)/shard_map/ppermute | solution.py:14
  84.7 9.1 %collective-permute-done.2 = bf16[512,384]{0,1:T(8,128)(2,1)} collective-permute-done((bf16[512,384]{0,1:T(8,128)(2,1)}, bf16[512,384]{0,1:T(8,128)(2,1)}, u32[]{:S(2)}, u32[]{:S(2)}) %collective-permute-start.2) | collective-permute-done | bytes 393248 | tf_op jit(solution)/shard_map/ppermute | solution.py:14
  106.3 4.2 conditional.10
  112.2 4.2 conditional.11
  119.8 4.2 conditional.13
  129.9 1.7 convolution_convert_fusion.1
  132.0 104.9 %all-reduce.4.cloned.1.call-done = bf16[512,1408]{1,0:T(8,128)(2,1)} async-done(((bf16[512,1408]{1,0:T(8,128)(2,1)}), bf16[512,1408]{1,0:T(8,128)(2,1)}) %all-reduce.4.cloned.1.call-update) | async-done | bytes 1441808 | tf_op jit(solution)/shard_map/psum | solution.py:127
  236.9 2.4 fusion.79
  240.2 9.7 %convolution_convert_fusion = bf16[512,1408]{1,0:T(8,128)(2,1)} fusion(bf16[768,1408]{1,0:T(8,128)(2,1)S(1)} %copy-done, bf16[1408,768]{1,0:T(8,128)(2,1)} %param.37, bf16[512,1408]{1,0:T(8,128)(2,1)} %all-reduce.4.cloned.1.call-done, bf16[512,1408]{1,0:T(8,128)(2,1)} %param.29, f32[1408]{0:T(1024)S(1)} %copy-done.10, f32[1408]{0:T(1024)S(1)} %copy-done.11, ...), kind=kOutput, calls=%fused_computation.123 | convolution fusion | flops 2246639616 | bytes 8666112 | tf_op jit(solution)/shard_map/dot_general | solution.py:132
  250.5 105.5 %all-reduce.6.cloned.1.call-done = bf16[512,1408]{1,0:T(8,128)(2,1)} async-done(((bf16[512,1408]{1,0:T(8,128)(2,1)}), bf16[512,1408]{1,0:T(8,128)(2,1)}) %all-reduce.6.cloned.1.call-update) | async-done | bytes 1441808 | tf_op jit(solution)/shard_map/psum | solution.py:133
  356.1 4.0 add_convert_fusion
  360.1 3.6 reshape.409
  364.8 4.1 abs_reduce_fusion
  370.6 17.1 %collective-permute-start.9 = (f32[48]{0:T(128)S(1)}, f32[48]{0:T(128)S(1)}, u32[]{:S(2)}, u32[]{:S(2)}) collective-permute-start(f32[48]{0:T(128)S(1)} %pad_maximum_fusion.1), channel_id=1, source_target_pairs={{0,2},{1,3},{2,0},{3,1},{4,6},{5,7},{6,4},{7,5},{8,10},{9,11},{10,... | collective-permute-start | bytes 584 | tf_op jit(solution)/shard_map/ppermute | solution.py:30
  389.4 2.5 collective-permute-start.10
  391.8 2.0 collective-permute-done.10
  395.5 6.0 %collective-permute-done.11 = f32[48]{0:T(128)S(1)} collective-permute-done((f32[48]{0:T(128)S(1)}, f32[48]{0:T(128)S(1)}, u32[]{:S(2)}, u32[]{:S(2)}) %collective-permute-start.11) | collective-permute-done | bytes 224 | tf_op jit(solution)/shard_map/ppermute | solution.py:30
  402.0 3.2 collective-permute-done.12
  405.4 1.9 collective-permute-start.13
  407.3 3.2 collective-permute-done.13
  412.0 2.2 collective-permute-done.14
  414.4 2.1 collective-permute-start.15
  416.4 3.0 collective-permute-done.15
  (146 shorter events, 57.0 us)
Async XLA Ops:
  8.0 232.2 %copy-start = (bf16[768,1408]{1,0:T(8,128)(2,1)S(1)}, bf16[768,1408]{1,0:T(8,128)(2,1)}, u32[]{:S(2)}) copy-start(bf16[768,1408]{1,0:T(8,128)(2,1)} %param.38) | copy-start | bytes 6488068
  8.0 3.1 copy-start.8
  8.0 228.9 %all-reduce.4.cloned.1.call-start = ((), (), s32[]{:S(2)}) async-start(), calls=%async_computation | async-start | bytes 2883584 | tf_op jit(solution)/shard_map/psum | solution.py:127
  8.1 2.5 copy-start.1
  8.1 3.1 copy-start.9
  14.9 33.7 %collective-permute-start.7 = (bf16[512,384]{0,1:T(8,128)(2,1)}, bf16[512,384]{0,1:T(8,128)(2,1)}, u32[]{:S(2)}, u32[]{:S(2)}) collective-permute-start(bf16[512,384]{0,1:T(8,128)(2,1)} %fusion.135), channel_id=1, source_target_pairs={{0,8},{8,16},{16,24},{24,32},{32,40},{40,48},{48,56},{56,64},{64,7... | collective-permute-start | bytes 1179656 | tf_op jit(solution)/shard_map/ppermute | solution.py:14
  24.0 34.8 %collective-permute-start.6 = (bf16[512,384]{0,1:T(8,128)(2,1)}, bf16[512,384]{0,1:T(8,128)(2,1)}, u32[]{:S(2)}, u32[]{:S(2)}) collective-permute-start(bf16[512,384]{0,1:T(8,128)(2,1)} %fusion.135), channel_id=1, source_target_pairs={{8,0},{16,8},{24,16},{32,24},{40,32},{48,40},{56,48},{64,56},{72,6... | collective-permute-start | bytes 1179656 | tf_op jit(solution)/shard_map/ppermute | solution.py:14
  28.4 33.7 %collective-permute-start.5 = (bf16[512,384]{0,1:T(8,128)(2,1)}, bf16[512,384]{0,1:T(8,128)(2,1)}, u32[]{:S(2)}, u32[]{:S(2)}) collective-permute-start(bf16[512,384]{0,1:T(8,128)(2,1)} %fusion.135), channel_id=1, source_target_pairs={{0,16},{8,24},{16,32},{24,40},{32,48},{40,56},{48,64},{56,72},{64,... | collective-permute-start | bytes 1179656 | tf_op jit(solution)/shard_map/ppermute | solution.py:14
  30.3 39.5 %collective-permute-start.4 = (bf16[512,384]{0,1:T(8,128)(2,1)}, bf16[512,384]{0,1:T(8,128)(2,1)}, u32[]{:S(2)}, u32[]{:S(2)}) collective-permute-start(bf16[512,384]{0,1:T(8,128)(2,1)} %fusion.135), channel_id=1, source_target_pairs={{16,0},{24,8},{32,16},{40,24},{48,32},{56,40},{64,48},{72,56},{80,... | collective-permute-start | bytes 1179656 | tf_op jit(solution)/shard_map/ppermute | solution.py:14
  36.4 44.5 %collective-permute-start.3 = (bf16[512,384]{0,1:T(8,128)(2,1)}, bf16[512,384]{0,1:T(8,128)(2,1)}, u32[]{:S(2)}, u32[]{:S(2)}) collective-permute-start(bf16[512,384]{0,1:T(8,128)(2,1)} %fusion.135), channel_id=1, source_target_pairs={{0,24},{8,32},{16,40},{24,48},{32,56},{40,64},{48,72},{56,80},{64,... | collective-permute-start | bytes 1179656 | tf_op jit(solution)/shard_map/ppermute | solution.py:14
  48.7 45.1 %collective-permute-start.2 = (bf16[512,384]{0,1:T(8,128)(2,1)}, bf16[512,384]{0,1:T(8,128)(2,1)}, u32[]{:S(2)}, u32[]{:S(2)}) collective-permute-start(bf16[512,384]{0,1:T(8,128)(2,1)} %fusion.135), channel_id=1, source_target_pairs={{24,0},{32,8},{40,16},{48,24},{56,32},{64,40},{72,48},{80,56},{88,... | collective-permute-start | bytes 1179656 | tf_op jit(solution)/shard_map/ppermute | solution.py:14
  58.8 38.8 %collective-permute-start.1 = (bf16[512,384]{0,1:T(8,128)(2,1)}, bf16[512,384]{0,1:T(8,128)(2,1)}, u32[]{:S(2)}, u32[]{:S(2)}) collective-permute-start(bf16[512,384]{0,1:T(8,128)(2,1)} %fusion.135), channel_id=1, source_target_pairs={{0,32},{8,40},{16,48},{24,56},{32,64},{40,72},{48,80},{56,88},{64,... | collective-permute-start | bytes 1179656 | tf_op jit(solution)/shard_map/ppermute | solution.py:14
  62.1 39.3 %collective-permute-start = (bf16[512,384]{0,1:T(8,128)(2,1)}, bf16[512,384]{0,1:T(8,128)(2,1)S(1)}, u32[]{:S(2)}, u32[]{:S(2)}) collective-permute-start(bf16[512,384]{0,1:T(8,128)(2,1)} %fusion.135), channel_id=1, source_target_pairs={{32,0},{40,8},{48,16},{56,24},{64,32},{72,40},{80,48},{88,56},{96,... | collective-permute-start | bytes 1179656 | tf_op jit(solution)/shard_map/ppermute | solution.py:14
  101.4 3.1 copy-start.5
  128.9 1.0 copy-start.4
  131.7 224.4 %all-reduce.6.cloned.1.call-start = ((), (), s32[]{:S(2)}) async-start(), calls=%async_computation.1 | async-start | bytes 2883584 | tf_op jit(solution)/shard_map/psum | solution.py:133
  236.9 2.4 copy-start.2
  236.9 2.7 copy-start.3
  239.3 0.9 copy-start.10
  239.3 0.9 copy-start.11
  250.0 114.8 %all-gather.2.cloned.1.call-start = ((), (), s32[]{:S(2)}) async-start(), calls=%async_computation.2 | async-start | bytes 5947392 | tf_op jit(solution)/shard_map/all_gather | solution.py:139
  363.7 5.2 %copy-start.6 = (s32[128]{0:T(128)S(1)}, s32[128]{0:T(128)}, u32[]{:S(2)}) copy-start(s32[128]{0:T(128)} %param.30) | copy-start | bytes 1540
  369.2 1.2 collective-permute-start.8
  370.6 18.6 %collective-permute-start.9 = (f32[48]{0:T(128)S(1)}, f32[48]{0:T(128)S(1)}, u32[]{:S(2)}, u32[]{:S(2)}) collective-permute-start(f32[48]{0:T(128)S(1)} %pad_maximum_fusion.1), channel_id=1, source_target_pairs={{0,2},{1,3},{2,0},{3,1},{4,6},{5,7},{6,4},{7,5},{8,10},{9,11},{10,... | collective-permute-start | bytes 584 | tf_op jit(solution)/shard_map/ppermute | solution.py:30
  389.4 4.5 %collective-permute-start.10 = (f32[48]{0:T(128)S(1)}, f32[48]{0:T(128)S(1)}, u32[]{:S(2)}, u32[]{:S(2)}) collective-permute-start(f32[48]{0:T(128)S(1)} %pad_maximum_fusion.2), channel_id=1, source_target_pairs={{0,4},{1,5},{2,6},{3,7},{4,0},{5,1},{6,2},{7,3},{8,12},{9,13},{10,... | collective-permute-start | bytes 584 | tf_op jit(solution)/shard_map/ppermute | solution.py:30
  394.0 7.5 %collective-permute-start.11 = (f32[48]{0:T(128)S(1)}, f32[48]{0:T(128)S(1)}, u32[]{:S(2)}, u32[]{:S(2)}) collective-permute-start(f32[48]{0:T(128)S(1)} %pad_maximum_fusion.3), channel_id=1, source_target_pairs={{0,8},{8,0},{16,24},{24,16},{32,40},{40,32},{48,56},{56,48},{64,72... | collective-permute-start | bytes 584 | tf_op jit(solution)/shard_map/ppermute | solution.py:30
  401.6 3.6 collective-permute-start.12
  405.4 5.1 %collective-permute-start.13 = (f32[48]{0:T(128)S(1)}, f32[48]{0:T(128)S(1)}, u32[]{:S(2)}, u32[]{:S(2)}) collective-permute-start(f32[48]{0:T(128)S(1)} %pad_maximum_fusion.5), channel_id=1, source_target_pairs={{0,32},{8,40},{16,48},{24,56},{32,0},{40,8},{48,16},{56,24},{64,96... | collective-permute-start | bytes 584 | tf_op jit(solution)/shard_map/ppermute | solution.py:30
  410.6 3.6 collective-permute-start.14
  414.4 5.1 %collective-permute-start.15 = (f32[48]{0:T(128)S(1)}, f32[48]{0:T(128)S(1)}, u32[]{:S(2)}, u32[]{:S(2)}) collective-permute-start(f32[48]{0:T(128)S(1)} %pad_maximum_fusion.7), channel_id=1, source_target_pairs={{0,128},{8,136},{16,144},{24,152},{32,160},{40,168},{48,176},{56,1... | collective-permute-start | bytes 584 | tf_op jit(solution)/shard_map/ppermute | solution.py:30
  420.0 0.9 copy-start.7
Sparse Core Ops, SparseCore 0:
  131.8 105.0 all-reduce.3
  250.1 105.9 all-reduce.5
Sparse Core Ops, SparseCore 1:
  253.9 110.8 all-gather.1

commit v2 on v1

--- a/solution.py
+++ b/solution.py
@@ -33,6 +33,12 @@
             )
             step *= 2
     return both[:split], both[split:]
+
+
+def gather_rows(x, n_head):
+    spread = jnp.broadcast_to(x[None], (n_head,) + x.shape)
+    got = lax.all_to_all(spread, "head", 0, 0, tiled=True)
+    return got.reshape((n_head * x.shape[0],) + x.shape[1:])
 
 
 def layer_norm(x, gain, bias):
@@ -123,15 +129,21 @@
     top, total, acc = state
     attn = (acc / total[..., None]).astype(jnp.bfloat16)
     attn = jnp.transpose(attn, (1, 0, 2)).reshape(rows, local_heads * HD)
-    attn_part = jnp.dot(attn, out_weight, preferred_element_type=jnp.float32)
-    h_one = x_in + lax.psum(attn_part.astype(jnp.bfloat16), "head").astype(jnp.float32)
-    n_two = layer_norm(h_one, ln2_gain, ln2_bias).astype(jnp.bfloat16)
+    n_head = lax.axis_size("head")
+    share = rows // n_head
+    width = x_in.shape[1]
+    attn_rows = lax.all_to_all(attn, "head", 0, 1, tiled=True)
+    full_out_weight = lax.all_gather(out_weight, "head", axis=0, tiled=True)
+    x_mine = lax.dynamic_slice_in_dim(x_in, lax.axis_index("head") * share, share, 0)
+    h_one = x_mine + jnp.dot(attn_rows, full_out_weight, preferred_element_type=jnp.float32)
+    n_two = gather_rows(layer_norm(h_one, ln2_gain, ln2_bias).astype(jnp.bfloat16), n_head)
     hidden = jax.nn.gelu(
         jnp.dot(n_two, fc1_weight, preferred_element_type=jnp.float32), approximate=False
     ).astype(jnp.bfloat16)
-    mlp_part = jnp.dot(hidden, fc2_weight, preferred_element_type=jnp.float32)
-    layer = (h_one + lax.psum(mlp_part.astype(jnp.bfloat16), "head").astype(jnp.float32)).astype(
-        jnp.bfloat16
+    mlp_part = jnp.dot(hidden, fc2_weight, preferred_element_type=jnp.float32).astype(jnp.bfloat16)
+    pieces = lax.all_to_all(mlp_part.reshape(n_head, share, width), "head", 0, 0, tiled=True)
+    layer = gather_rows(
+        (h_one + jnp.sum(pieces.astype(jnp.float32), axis=0)).astype(jnp.bfloat16), n_head
     )
     grouped = layer.reshape(rows // 4, 4 * layer.shape[1])
     proj = jnp.dot(

time: 429 us -> 444 us (1.035); the launches traced: 428 us -> 438 us
  waiting for transfers between devices: 244 us -> 62.3 us
  blocking collectives: 0 us -> 160 us
  starting transfers between devices: 69.7 us -> 98.9 us
    psum x2 -> x0, waiting for transfers between devices: 210 us -> none  [the longest x1 106 us: per_device(): lax.psum(mlp_part.astype(jnp.bfloat16), 'head').astype(jnp.float32)]
    all_to_all x0 -> x3, blocking collectives: none -> 160 us  [the longest x2 91 us: gather_rows(): got = lax.all_to_all(spread, 'head', 0, 0, tiled=True)]
    ppermute x8, waiting for transfers between devices: 9.12 us -> 37.4 us  [passed_along(): return lax.ppermute(x, axis, pairs)]
    ppermute x8, starting transfers between devices: 26.7 us -> 37.3 us  [butterfly(): other = lax.ppermute(both, axis, pairs)]
    all_gather x1, starting transfers between devices: 0.04 us -> 9.91 us  [per_device(): lax.all_gather(proj_weight, 'blk', axis=0, tiled=True)]
    all_to_all x0 -> x1, starting transfers between devices: none -> 7.06 us  [per_device(): attn_rows = lax.all_to_all(attn, 'head', 0, 1, tiled=True)]
  transfers between devices with their start and end apart: 19 -> 19, of which waited for: 12 -> 11; matrix products, arithmetic and copies ran while one was open for 5% -> 16% of each run, Pallas kernels for 0% -> 0%
where the time goes in v2:
time: 444 us; the launch traced here: 438 us
  blocking collectives  160 us (36%)
  starting transfers between devices  98.9 us (22%)
  waiting for transfers between devices  62.3 us (14%)
  other arithmetic  37.8 us (9%)
  between operations  36.5 us (8%)
  matrix products  26.8 us (6%)
  local copies, waits for them, and re-layouts  14.8 us (3%)
    all_to_all x2, blocking collectives, gather_rows(): got = lax.all_to_all(spread, 'head', 0, 0, tiled=True)  91 us
    all_to_all x1, blocking collectives, per_device(): lax.all_to_all(mlp_part.reshape(n_head, share, width), 'head', 0, 0, tile...  69 us
    ppermute x8, starting transfers between devices, passed_along(): return lax.ppermute(x, axis, pairs)  44.7 us
    ppermute x8, waiting for transfers between devices, passed_along(): return lax.ppermute(x, axis, pairs)  37.4 us
    ppermute x8, starting transfers between devices, butterfly(): other = lax.ppermute(both, axis, pairs)  37.3 us
    ppermute x8, waiting for transfers between devices, butterfly(): other = lax.ppermute(both, axis, pairs)  24.2 us
    reduce_max x8, other arithmetic, fold_block(): touches = (jnp.min(ipiece) <= own_high) & (jnp.max(ipiece) >= own_low)  10.9 us
    all_gather x1, starting transfers between devices, per_device(): lax.all_gather(proj_weight, 'blk', axis=0, tiled=True)  9.91 us
  transfers between devices with their start and end apart: 19, of which 11 were waited for; matrix products, arithmetic and copies ran while one was open for 16% of the time, Pallas kernels for 0%

profile of v2, /device:TPU:2, one launch (start us, length us, event | category | flops | bytes accessed | tf_op | source)
XLA Modules:
  0.0 437.6 jit_solution(4019858909612102725)
XLA Ops:
  14.0 9.1 %collective-permute-start.7 = (bf16[512,384]{0,1:T(8,128)(2,1)S(1)}, bf16[512,384]{0,1:T(8,128)(2,1)}, u32[]{:S(2)}, u32[]{:S(2)}) collective-permute-start(bf16[512,384]{0,1:T(8,128)(2,1)S(1)} %fusion.123), channel_id=1, source_target_pairs={{0,8},{8,16},{16,24},{24,32},{32,40},{40,48},{48,56},{56,64},{64,7... | collective-permute-start | bytes 1179656 | tf_op jit(solution)/shard_map/ppermute | solution.py:14
  23.1 4.3 collective-permute-start.6
  29.3 6.0 %collective-permute-start.4 = (bf16[512,384]{0,1:T(8,128)(2,1)S(1)}, bf16[512,384]{0,1:T(8,128)(2,1)}, u32[]{:S(2)}, u32[]{:S(2)}) collective-permute-start(bf16[512,384]{0,1:T(8,128)(2,1)S(1)} %fusion.123), channel_id=1, source_target_pairs={{16,0},{24,8},{32,16},{40,24},{48,32},{56,40},{64,48},{72,56},{80,... | collective-permute-start | bytes 1179656 | tf_op jit(solution)/shard_map/ppermute | solution.py:14
  35.4 4.3 collective-permute-start.3
  42.8 4.8 %conditional.9 = (f32[2,512]{1,0:T(2,128)}, f32[2,512]{1,0:T(2,128)S(1)}, f32[2,512,88]{1,2,0:T(8,128)S(1)}) conditional(s32[]{:T(128)} %convert_element_type.176, () %tuple.65, (s32[128,4]{1,0:T(8,128)S(1)}, bf16[1,512,176]{1,2,0:T(8,128)(2,1)S(1)}, bf16[512,2,88]{0,2,1:T(8,128)(2,1)S(1)}, bf16[1,512,176]{1,2,0:T(8,128)(2,1)S(1)}) %tuple.160), branch_computations={%region_20.21_spmd, %region_21.24_spmd} | conditional | flops 190672896 | bytes 8292376 | solution.py:107
  47.7 10.7 %collective-permute-start.2 = (bf16[512,384]{0,1:T(8,128)(2,1)S(1)}, bf16[512,384]{0,1:T(8,128)(2,1)}, u32[]{:S(2)}, u32[]{:S(2)}) collective-permute-start(bf16[512,384]{0,1:T(8,128)(2,1)S(1)} %fusion.123), channel_id=1, source_target_pairs={{24,0},{32,8},{40,16},{48,24},{56,32},{64,40},{72,48},{80,56},{88,... | collective-permute-start | bytes 1179656 | tf_op jit(solution)/shard_map/ppermute | solution.py:14
  59.8 11.9 %collective-permute-done.6 = bf16[512,384]{0,1:T(8,128)(2,1)} collective-permute-done((bf16[512,384]{0,1:T(8,128)(2,1)S(1)}, bf16[512,384]{0,1:T(8,128)(2,1)}, u32[]{:S(2)}, u32[]{:S(2)}) %collective-permute-start.6) | collective-permute-done | bytes 393248 | tf_op jit(solution)/shard_map/ppermute | solution.py:14
  71.7 5.1 %collective-permute-start.1 = (bf16[512,384]{0,1:T(8,128)(2,1)S(1)}, bf16[512,384]{0,1:T(8,128)(2,1)}, u32[]{:S(2)}, u32[]{:S(2)}) collective-permute-start(bf16[512,384]{0,1:T(8,128)(2,1)S(1)} %fusion.123), channel_id=1, source_target_pairs={{0,32},{8,40},{16,48},{24,56},{32,64},{40,72},{48,80},{56,88},{64,... | collective-permute-start | bytes 1179656 | tf_op jit(solution)/shard_map/ppermute | solution.py:14
  78.2 3.1 collective-permute-start
  93.8 3.2 collective-permute-done.3
  100.8 22.2 %collective-permute-done.2 = bf16[512,384]{0,1:T(8,128)(2,1)} collective-permute-done((bf16[512,384]{0,1:T(8,128)(2,1)S(1)}, bf16[512,384]{0,1:T(8,128)(2,1)}, u32[]{:S(2)}, u32[]{:S(2)}) %collective-permute-start.2) | collective-permute-done | bytes 393248 | tf_op jit(solution)/shard_map/ppermute | solution.py:14
  136.2 4.2 conditional.10
  142.1 4.2 conditional.11
  148.1 4.2 conditional.12
  156.0 4.2 conditional.14
  164.4 7.1 %all-to-all-start = ((bf16[8,64,176]{2,1,0:T(8,128)(2,1)}), bf16[8,64,176]{2,1,0:T(8,128)(2,1)S(1)}, u32[]{:S(2)}, u32[]{:S(2)}) async-start(bf16[8,64,176]{2,1,0:T(8,128)(2,1)} %all_to_all.23), calls=%async_computation | async-start | bytes 524288 | tf_op jit(solution)/shard_map/all_to_all | solution.py:135
  171.5 9.9 %all-gather.5.cloned.1.call-start = ((), (), s32[]{:S(2)}) async-start(), calls=%async_computation.5 | async-start | bytes 5947392 | tf_op jit(solution)/shard_map/all_gather | solution.py:151
  181.4 3.1 convert_element_type.154
  185.0 3.0 fusion.185
  188.5 42.3 %all_to_all.34 = bf16[8,64,1408]{2,1,0:T(8,128)(2,1)} all-to-all(bf16[8,64,1408]{2,1,0:T(8,128)(2,1)S(1)} %broadcast_in_dim.224), channel_id=1, replica_groups=mesh['blk'=32,'head'=8] {'head'}, dimensions={0} | all-to-all | bytes 2883584 | tf_op jit(solution)/shard_map/all_to_all | solution.py:40
  230.8 9.5 %convolution_convert_fusion = bf16[512,1408]{1,0:T(8,128)(2,1)} fusion(bf16[768,1408]{1,0:T(8,128)(2,1)S(1)} %copy-done, bf16[512,1408]{1,0:T(8,128)(2,1)} %bitcast.94, bf16[1408,768]{1,0:T(8,128)(2,1)} %param.37), kind=kOutput, calls=%fused_computation.118 | convolution fusion | flops 2240872448 | bytes 7208960 | tf_op jit(solution)/shard_map/dot_general | solution.py:143
  240.3 69.0 %all_to_all.35 = bf16[8,64,1408]{2,1,0:T(8,128)(2,1)S(1)} all-to-all(bf16[8,64,1408]{2,1,0:T(8,128)(2,1)} %bitcast.95), channel_id=1, replica_groups=mesh['blk'=32,'head'=8] {'head'}, dimensions={0} | all-to-all | bytes 2883584 | tf_op jit(solution)/shard_map/all_to_all | solution.py:144
  309.7 48.7 %all_to_all.36 = bf16[8,64,1408]{2,1,0:T(8,128)(2,1)} all-to-all(bf16[8,64,1408]{2,1,0:T(8,128)(2,1)S(1)} %broadcast_in_dim.225), channel_id=1, replica_groups=mesh['blk'=32,'head'=8] {'head'}, dimensions={0} | all-to-all | bytes 2883584 | tf_op jit(solution)/shard_map/all_to_all | solution.py:40
  358.4 3.6 reshape_reshape.3
  362.0 4.1 abs_reduce_fusion
  368.0 3.4 collective-permute-done.9
  371.6 4.5 %collective-permute-done.10 = f32[48]{0:T(128)S(1)} collective-permute-done((f32[48]{0:T(128)S(1)}, f32[48]{0:T(128)S(1)}, u32[]{:S(2)}, u32[]{:S(2)}) %collective-permute-start.10) | collective-permute-done | bytes 224 | tf_op jit(solution)/shard_map/ppermute | solution.py:30
  376.2 10.5 %collective-permute-start.11 = (f32[48]{0:T(128)S(1)}, f32[48]{0:T(128)S(1)}, u32[]{:S(2)}, u32[]{:S(2)}) collective-permute-start(f32[48]{0:T(128)S(1)} %pad_maximum_fusion.3), channel_id=1, source_target_pairs={{0,8},{8,0},{16,24},{24,16},{32,40},{40,32},{48,56},{56,48},{64,72... | collective-permute-start | bytes 584 | tf_op jit(solution)/shard_map/ppermute | solution.py:30
  388.4 3.6 collective-permute-done.12
  392.2 5.0 %collective-permute-done.13 = f32[48]{0:T(128)S(1)} collective-permute-done((f32[48]{0:T(128)S(1)}, f32[48]{0:T(128)S(1)}, u32[]{:S(2)}, u32[]{:S(2)}) %collective-permute-start.13) | collective-permute-done | bytes 224 | tf_op jit(solution)/shard_map/ppermute | solution.py:30
  397.4 3.6 collective-permute-done.14
  401.1 26.4 %collective-permute-start.15 = (f32[48]{0:T(128)S(1)}, f32[48]{0:T(128)S(1)}, u32[]{:S(2)}, u32[]{:S(2)}) collective-permute-start(f32[48]{0:T(128)S(1)} %pad_maximum_fusion.7), channel_id=1, source_target_pairs={{0,128},{8,136},{16,144},{24,152},{32,160},{40,168},{48,176},{56,1... | collective-permute-start | bytes 584 | tf_op jit(solution)/shard_map/ppermute | solution.py:30
  (156 shorter events, 63.7 us)
Async XLA Ops:
  7.2 223.7 %copy-start = (bf16[768,1408]{1,0:T(8,128)(2,1)S(1)}, bf16[768,1408]{1,0:T(8,128)(2,1)}, u32[]{:S(2)}) copy-start(bf16[768,1408]{1,0:T(8,128)(2,1)} %param.38) | copy-start | bytes 6488068
  7.2 3.9 copy-start.7
  7.2 3.9 copy-start.6
  7.2 177.8 %all-gather.3.cloned.1.call-start = ((), (), s32[]{:S(2)}) async-start(), calls=%async_computation.4 | async-start | bytes 4460544 | tf_op jit(solution)/shard_map/all_gather | solution.py:136
  8.8 1.8 copy-start.1
  14.0 33.7 %collective-permute-start.7 = (bf16[512,384]{0,1:T(8,128)(2,1)S(1)}, bf16[512,384]{0,1:T(8,128)(2,1)}, u32[]{:S(2)}, u32[]{:S(2)}) collective-permute-start(bf16[512,384]{0,1:T(8,128)(2,1)S(1)} %fusion.123), channel_id=1, source_target_pairs={{0,8},{8,16},{16,24},{24,32},{32,40},{40,48},{48,56},{56,64},{64,7... | collective-permute-start | bytes 1179656 | tf_op jit(solution)/shard_map/ppermute | solution.py:14
  23.1 48.7 %collective-permute-start.6 = (bf16[512,384]{0,1:T(8,128)(2,1)S(1)}, bf16[512,384]{0,1:T(8,128)(2,1)}, u32[]{:S(2)}, u32[]{:S(2)}) collective-permute-start(bf16[512,384]{0,1:T(8,128)(2,1)S(1)} %fusion.123), channel_id=1, source_target_pairs={{8,0},{16,8},{24,16},{32,24},{40,32},{48,40},{56,48},{64,56},{72,6... | collective-permute-start | bytes 1179656 | tf_op jit(solution)/shard_map/ppermute | solution.py:14
  27.4 50.8 %collective-permute-start.5 = (bf16[512,384]{0,1:T(8,128)(2,1)S(1)}, bf16[512,384]{0,1:T(8,128)(2,1)}, u32[]{:S(2)}, u32[]{:S(2)}) collective-permute-start(bf16[512,384]{0,1:T(8,128)(2,1)S(1)} %fusion.123), channel_id=1, source_target_pairs={{0,16},{8,24},{16,32},{24,40},{32,48},{40,56},{48,64},{56,72},{64,... | collective-permute-start | bytes 1179656 | tf_op jit(solution)/shard_map/ppermute | solution.py:14
  29.3 53.4 %collective-permute-start.4 = (bf16[512,384]{0,1:T(8,128)(2,1)S(1)}, bf16[512,384]{0,1:T(8,128)(2,1)}, u32[]{:S(2)}, u32[]{:S(2)}) collective-permute-start(bf16[512,384]{0,1:T(8,128)(2,1)S(1)} %fusion.123), channel_id=1, source_target_pairs={{16,0},{24,8},{32,16},{40,24},{48,32},{56,40},{64,48},{72,56},{80,... | collective-permute-start | bytes 1179656 | tf_op jit(solution)/shard_map/ppermute | solution.py:14
  35.4 61.6 %collective-permute-start.3 = (bf16[512,384]{0,1:T(8,128)(2,1)S(1)}, bf16[512,384]{0,1:T(8,128)(2,1)}, u32[]{:S(2)}, u32[]{:S(2)}) collective-permute-start(bf16[512,384]{0,1:T(8,128)(2,1)S(1)} %fusion.123), channel_id=1, source_target_pairs={{0,24},{8,32},{16,40},{24,48},{32,56},{40,64},{48,72},{56,80},{64,... | collective-permute-start | bytes 1179656 | tf_op jit(solution)/shard_map/ppermute | solution.py:14
  47.7 75.3 %collective-permute-start.2 = (bf16[512,384]{0,1:T(8,128)(2,1)S(1)}, bf16[512,384]{0,1:T(8,128)(2,1)}, u32[]{:S(2)}, u32[]{:S(2)}) collective-permute-start(bf16[512,384]{0,1:T(8,128)(2,1)S(1)} %fusion.123), channel_id=1, source_target_pairs={{24,0},{32,8},{40,16},{48,24},{56,32},{64,40},{72,48},{80,56},{88,... | collective-permute-start | bytes 1179656 | tf_op jit(solution)/shard_map/ppermute | solution.py:14
  71.7 55.1 %collective-permute-start.1 = (bf16[512,384]{0,1:T(8,128)(2,1)S(1)}, bf16[512,384]{0,1:T(8,128)(2,1)}, u32[]{:S(2)}, u32[]{:S(2)}) collective-permute-start(bf16[512,384]{0,1:T(8,128)(2,1)S(1)} %fusion.123), channel_id=1, source_target_pairs={{0,32},{8,40},{16,48},{24,56},{32,64},{40,72},{48,80},{56,88},{64,... | collective-permute-start | bytes 1179656 | tf_op jit(solution)/shard_map/ppermute | solution.py:14
  78.2 52.4 %collective-permute-start = (bf16[512,384]{0,1:T(8,128)(2,1)S(1)}, bf16[512,384]{0,1:T(8,128)(2,1)}, u32[]{:S(2)}, u32[]{:S(2)}) collective-permute-start(bf16[512,384]{0,1:T(8,128)(2,1)S(1)} %fusion.123), channel_id=1, source_target_pairs={{32,0},{40,8},{48,16},{56,24},{64,32},{72,40},{80,48},{88,56},{96,... | collective-permute-start | bytes 1179656 | tf_op jit(solution)/shard_map/ppermute | solution.py:14
  164.4 20.1 %all-to-all-start = ((bf16[8,64,176]{2,1,0:T(8,128)(2,1)}), bf16[8,64,176]{2,1,0:T(8,128)(2,1)S(1)}, u32[]{:S(2)}, u32[]{:S(2)}) async-start(bf16[8,64,176]{2,1,0:T(8,128)(2,1)} %all_to_all.23), calls=%async_computation | async-start | bytes 524288 | tf_op jit(solution)/shard_map/all_to_all | solution.py:135
  171.5 190.5 %all-gather.5.cloned.1.call-start = ((), (), s32[]{:S(2)}) async-start(), calls=%async_computation.5 | async-start | bytes 5947392 | tf_op jit(solution)/shard_map/all_gather | solution.py:151
  185.0 3.3 copy-start.2
  185.0 3.3 copy-start.3
  362.0 4.1 copy-start.4
  366.4 1.2 collective-permute-start.8
  367.8 3.6 collective-permute-start.9
  371.6 4.5 %collective-permute-start.10 = (f32[48]{0:T(128)S(1)}, f32[48]{0:T(128)S(1)}, u32[]{:S(2)}, u32[]{:S(2)}) collective-permute-start(f32[48]{0:T(128)S(1)} %pad_maximum_fusion.2), channel_id=1, source_target_pairs={{0,4},{1,5},{2,6},{3,7},{4,0},{5,1},{6,2},{7,3},{8,12},{9,13},{10,... | collective-permute-start | bytes 584 | tf_op jit(solution)/shard_map/ppermute | solution.py:30
  376.2 12.0 %collective-permute-start.11 = (f32[48]{0:T(128)S(1)}, f32[48]{0:T(128)S(1)}, u32[]{:S(2)}, u32[]{:S(2)}) collective-permute-start(f32[48]{0:T(128)S(1)} %pad_maximum_fusion.3), channel_id=1, source_target_pairs={{0,8},{8,0},{16,24},{24,16},{32,40},{40,32},{48,56},{56,48},{64,72... | collective-permute-start | bytes 584 | tf_op jit(solution)/shard_map/ppermute | solution.py:30
  388.4 3.6 collective-permute-start.12
  392.1 5.1 %collective-permute-start.13 = (f32[48]{0:T(128)S(1)}, f32[48]{0:T(128)S(1)}, u32[]{:S(2)}, u32[]{:S(2)}) collective-permute-start(f32[48]{0:T(128)S(1)} %pad_maximum_fusion.5), channel_id=1, source_target_pairs={{0,32},{8,40},{16,48},{24,56},{32,0},{40,8},{48,16},{56,24},{64,96... | collective-permute-start | bytes 584 | tf_op jit(solution)/shard_map/ppermute | solution.py:30
  397.4 3.6 collective-permute-start.14
  401.1 28.0 %collective-permute-start.15 = (f32[48]{0:T(128)S(1)}, f32[48]{0:T(128)S(1)}, u32[]{:S(2)}, u32[]{:S(2)}) collective-permute-start(f32[48]{0:T(128)S(1)} %pad_maximum_fusion.7), channel_id=1, source_target_pairs={{0,128},{8,136},{16,144},{24,152},{32,160},{40,168},{48,176},{56,1... | collective-permute-start | bytes 584 | tf_op jit(solution)/shard_map/ppermute | solution.py:30
  429.7 0.9 copy-start.5
Sparse Core Ops, SparseCore 0:
  9.8 119.7 all-gather.2
  181.6 148.0 all-gather.4
